TPU v7x, 512 devices: a whole 4x8x8 slice. The times are simulated.
512 devices in a mesh: shard: 128 (over y, z, core), tensor: 4 (over x).
Axes of the slice: x: 4, y: 8, z: 8, core: 2. Of those that a mesh axis runs over, the one named last changes fastest.
Arguments:
- big_grad: bfloat16 [32, 1280, 768], P(None, 'shard', 'tensor')
- big_weight: bfloat16 [32, 1280, 768], P(None, 'shard', 'tensor'), may hold values from -0.017944336 to 0.017944336
- big_moment: float32 [128, 768, 1280], P('shard', 'tensor'), may hold values from -6 to 6
- small_grad: bfloat16 [32, 1280, 192], P(None, 'shard')
- small_weight: bfloat16 [32, 1280, 192], P(None, 'shard'), may hold values from -0.15625 to 0.15625
- small_moment: float32 [128, 192, 1280], P('shard'), may hold values from -6 to 6
- owners: int32 [2, 32], replicated, may hold values from 0 to 127, as said below
- vec_parts: float32 [128, 43008], P('shard'), may hold values from -0.6 to 0.6
- vec_param: float32 [43008], P('shard'), may hold values from 0.5 to 1.5
- vec_first: float32 [43008], P('shard'), may hold values from -0.6 to 0.6
- vec_second: float32 [43008], P('shard'), may hold values from 0.01 to 1
Outputs:
- big_weight_new: bfloat16 [32, 1280, 768], P(None, 'shard', 'tensor')
- big_moment_new: float32 [128, 768, 1280], P('shard', 'tensor')
- small_weight_new: bfloat16 [32, 1280, 192], P(None, 'shard')
- small_moment_new: float32 [128, 192, 1280], P('shard')
- vec_param_new: float32 [43008], P('shard')
- vec_first_new: float32 [43008], P('shard')
- vec_second_new: float32 [43008], P('shard')
Inputs may be any that keep to these rules, and one draw needn't show every extreme that they name: `owners`: no shard index appears twice in the whole list (over both rows); each aligned group of four shard indices holds exactly one owner of each row; the first and the last shard index own a matrix.
All inputs are finite; a program needn't handle non-finite values.
Results may differ from a plain program's by a relative error of at most 0.0068.
Values may be sent and summed in bfloat16 or wider, within the bound.
No kernel may reach another device: no remote copies, remote signals or barrier semaphores. Data moves between devices by JAX's collectives and lax.ppermute only.
A program may use at most 64 MiB of HBM per device.

v0:
```python
import math
import jax
import jax.numpy as jnp
from jax import lax
from jax.sharding import PartitionSpec as P

D = 1280
ITERS = 2
newton_linear = 3.4445
newton_cubic = -4.775
newton_quintic = 2.0315
momentum_rate = 0.95
muon_rate = 0.05
weight_decay = 0.1
norm_epsilon = 1e-07
adam_rate = 0.004
first_decay = 0.9
second_decay = 0.95
adam_epsilon = 1e-08
first_correct = 0.99997343860111
second_correct = 0.99407947077967


def owner_table(owner_list, count):
    devices = lax.broadcasted_iota(jnp.int32, (count, owner_list.shape[0]), 0)
    return (devices == owner_list[None, :]).astype(jnp.bfloat16)


def route_rows(owner_map, pieces):
    flattened = pieces.reshape(pieces.shape[0], -1)
    routed = jnp.dot(owner_map, flattened, preferred_element_type=jnp.float32)
    return routed.astype(jnp.bfloat16).reshape((owner_map.shape[0],) + pieces.shape[1:])


def collect(owner_map, arrived):
    flattened = arrived.reshape(arrived.shape[0], -1)
    picked = lax.dot_general(
        owner_map, flattened, (((0,), (0,)), ((), ())), preferred_element_type=jnp.float32
    )
    return picked.astype(jnp.bfloat16).reshape((owner_map.shape[1],) + arrived.shape[1:])


def advance(arrived, moment, is_owner):
    gradient = arrived.T.astype(jnp.float32)
    renewed = momentum_rate * moment + gradient
    retained = jnp.where(is_owner, renewed, moment)
    blended = jnp.where(is_owner, gradient + momentum_rate * renewed, 0.0).astype(jnp.bfloat16).T
    return (retained, blended)


def normalized(field):
    values = field.astype(jnp.float32)
    squares = jnp.sum(values * values)
    return (values / (jnp.sqrt(squares) + norm_epsilon)).astype(jnp.bfloat16)


def gram_block(left_part, right_part):
    product = lax.dot_general(
        left_part, right_part, (((0,), (0,)), ((), ())), preferred_element_type=jnp.float32
    )
    return product.astype(jnp.bfloat16)


def poly_block(gram_part, gram_full):
    square = jnp.dot(gram_part, gram_full, preferred_element_type=jnp.float32)
    return (newton_cubic * gram_part.astype(jnp.float32) + newton_quintic * square).astype(
        jnp.bfloat16
    )


def newton_step(column_part, full_iterate, polynomial):
    product = lax.dot_general(
        full_iterate, polynomial, (((1,), (1,)), ((), ())), preferred_element_type=jnp.float32
    )
    return (newton_linear * column_part.astype(jnp.float32) + product).astype(jnp.bfloat16)


def small_newton(field):
    iterate = normalized(field)
    for iteration in range(ITERS):
        gram_full = gram_block(iterate, iterate)
        iterate = newton_step(iterate, iterate, poly_block(gram_full, gram_full))
    return iterate


def apply_update(weight, update):
    scale = 0.2 * math.sqrt(D)
    values = weight.astype(jnp.float32)
    return (
        values - muon_rate * (scale * update.astype(jnp.float32) + weight_decay * values)
    ).astype(jnp.bfloat16)


def gather_columns(column_part):
    return lax.all_gather(column_part, "tensor", axis=1, tiled=True)


def gather_gram(gram_part):
    return lax.all_gather(gram_part, "tensor", axis=0, tiled=True)


def per_device(
    big_grad,
    big_weight,
    big_moment,
    small_grad,
    small_weight,
    small_moment,
    owners,
    vec_parts,
    vec_param,
    vec_first,
    vec_second,
):
    shards = lax.axis_size("shard")
    shard_place = lax.axis_index("shard")
    column = lax.axis_index("tensor")
    block_width = big_grad.shape[2]
    rows_dev = big_grad.shape[1]
    matrices = big_grad.shape[0]
    joint_map = owner_table(jnp.concatenate([owners[0], owners[1]]), shards)
    joint_pieces = jnp.concatenate([big_grad, small_grad], axis=0)
    arrived = lax.all_to_all(
        route_rows(joint_map, joint_pieces), "shard", split_axis=0, concat_axis=1, tiled=True
    )[0]
    big_owner = jnp.any(owners[0] == shard_place)
    small_owner = jnp.any(owners[1] == shard_place)
    big_retained, big_blended = advance(arrived, big_moment[0], big_owner)
    small_retained, small_blended = advance(arrived, small_moment[0], small_owner)
    small_result = small_newton(small_blended)
    full_iterate = normalized(gather_columns(big_blended))
    for iteration in range(ITERS):
        owned_part = lax.dynamic_slice_in_dim(full_iterate, column * block_width, block_width, 1)
        gram_full = gather_gram(gram_block(owned_part, full_iterate))
        full_iterate = newton_step(full_iterate, full_iterate, poly_block(gram_full, gram_full))
    big_result = lax.dynamic_slice_in_dim(full_iterate, column * block_width, block_width, 1)
    own_result = jnp.where(big_owner, big_result, small_result)
    returned = lax.all_to_all(
        own_result.reshape(shards, rows_dev, block_width),
        "shard",
        split_axis=0,
        concat_axis=0,
        tiled=True,
    )
    picked = collect(joint_map, returned)
    big_weight_new = apply_update(big_weight, picked[:matrices])
    small_weight_new = apply_update(small_weight, picked[matrices:])
    grad_share = lax.psum_scatter(vec_parts[0], "shard", scatter_dimension=0, tiled=True)
    first_new = first_decay * vec_first + (1.0 - first_decay) * grad_share
    second_new = second_decay * vec_second + (1.0 - second_decay) * grad_share * grad_share
    param_new = vec_param - adam_rate * (first_new / first_correct) / (
        jnp.sqrt(second_new / second_correct) + adam_epsilon
    )
    return (
        big_weight_new,
        big_retained[None],
        small_weight_new,
        small_retained[None],
        param_new,
        first_new,
        second_new,
    )


def solution(mesh):
    return jax.shard_map(
        per_device,
        mesh=mesh,
        in_specs=(
            P(None, "shard", "tensor"),
            P(None, "shard", "tensor"),
            P("shard", "tensor", None),
            P(None, "shard", None),
            P(None, "shard", None),
            P("shard", None, None),
            P(),
            P("shard", None),
            P("shard"),
            P("shard"),
            P("shard"),
        ),
        out_specs=(
            P(None, "shard", "tensor"),
            P("shard", "tensor", None),
            P(None, "shard", None),
            P("shard", None, None),
            P("shard"),
            P("shard"),
            P("shard"),
        ),
        check_vma=False,
    )
```

profile of v0, /device:TPU:1, one launch (start us, length us, event | category | flops | bytes accessed | tf_op | source)
XLA Modules:
  0.0 395.7 jit_solution(8860446382771876976)
XLA Ops:
  8.0 0.8 slice_bitcast_fusion.1
  8.8 1.0 pad_maximum_fusion
  11.0 1.3 copy.34
  12.4 1.6 reshape.48
  13.9 18.4 %all-to-all-start = ((bf16[128,2,960]{2,1,0:T(2,128)(2,1)}), bf16[128,2,960]{2,1,0:T(2,128)(2,1)S(1)}, u32[]{:S(2)}, u32[]{:S(2)}) async-start(bf16[128,2,960]{2,1,0:T(2,128)(2,1)} %reshape.48), calls=%async_computation | async-start | bytes 1048576 | tf_op jit(solution)/shard_map/all_to_all | solution.py:123
  32.4 0.6 compare_reduce_fusion.1
  33.1 18.7 %all-to-all-done = bf16[128,2,960]{2,1,0:T(2,128)(2,1)S(1)} async-done(((bf16[128,2,960]{2,1,0:T(2,128)(2,1)}), bf16[128,2,960]{2,1,0:T(2,128)(2,1)S(1)}, u32[]{:S(2)}, u32[]{:S(2)}) %all-to-all-start) | async-done | bytes 491552 | tf_op jit(solution)/shard_map/all_to_all | solution.py:123
  51.8 0.8 reshape.49
  52.9 0.4 copy.35
  53.3 0.8 copy-done.2
  54.1 4.9 %fusion.15 = (f32[1,192,1280]{2,1,0:T(8,128)}, bf16[1280,192]{0,1:T(8,128)(2,1)}, f32[1,192,1280]{2,1,0:T(8,128)}, f32[]{:T(128)}, bf16[192,1280]{1,0:T(8,128)(2,1)S(1)}) fusion(f32[1,192,1280]{2,1,0:T(8,128)S(1)} %copy-done.2, f32[1280,192]{0,1:T(8,128)S(1)} %copy.35, pred[]{:T(512)} %get-tuple-element.21, f32[1,192,1280]{2,1,0:T(8,128)} %param.16, ...), kind=kLoop, calls=%fused_computation.37 | loop fusion | flops 4177919 | bytes 5898246 | tf_op jit(solution)/shard_map/broadcast_in_dim | solution.py:156
  59.0 28.6 %all-gather.4.cloned.1.call-done = bf16[1280,768]{0,1:T(8,128)(2,1)} async-done(((bf16[1280,192]{0,1:T(8,128)(2,1)}), bf16[1280,768]{0,1:T(8,128)(2,1)}) %all-gather.4.cloned.1.call-update) | async-done | bytes 1966096 | tf_op jit(solution)/shard_map/all_gather | solution.py:95
  87.6 3.3 fusion
  92.0 1.3 copy-done.1
  93.3 1.5 convolution_convert_fusion.3
  95.1 27.7 %all-gather.6.cloned.1.call-done = bf16[768,768]{1,0:T(8,128)(2,1)} async-done(((bf16[192,768]{1,0:T(8,128)(2,1)}), bf16[768,768]{1,0:T(8,128)(2,1)}) %all-gather.6.cloned.1.call-update) | async-done | bytes 1179664 | tf_op jit(solution)/shard_map/all_gather | solution.py:99
  122.8 6.0 %add_convert_fusion = bf16[1280,768]{0,1:T(8,128)(2,1)S(1)} fusion(bf16[1280,768]{0,1:T(8,128)(2,1)} %copy-done.1, bf16[768,768]{1,0:T(8,128)(2,1)} %all-gather.6.cloned.1.call-done), kind=kOutput, calls=%fused_computation.4 | convolution fusion | flops 2422800384 | bytes 5111808 | tf_op jit(solution)/shard_map/dot_general | solution.py:72
  128.8 1.5 convolution_convert_fusion.2
  131.4 0.5 fusion.2
  132.2 28.7 %all-gather.8.cloned.1.call-done = bf16[768,768]{1,0:T(8,128)(2,1)} async-done(((bf16[192,768]{1,0:T(8,128)(2,1)}), bf16[768,768]{1,0:T(8,128)(2,1)}) %all-gather.8.cloned.1.call-update) | async-done | bytes 1179664 | tf_op jit(solution)/shard_map/all_gather | solution.py:99
  160.8 7.5 %fusion.20 = f32[1280,768]{0,1:T(8,128)} fusion(bf16[1280,768]{0,1:T(8,128)(2,1)} %copy-done.9, bf16[768,768]{1,0:T(8,128)(2,1)} %all-gather.8.cloned.1.call-done), kind=kOutput, calls=%fused_computation.44 | convolution fusion | flops 2418868224 | bytes 7077888 | tf_op jit(solution)/shard_map/dot_general | solution.py:72
  168.3 2.4 fusion.4
  171.3 1.6 reshape.50
  172.9 16.4 %all-to-all-start.1 = ((bf16[128,2,960]{2,1,0:T(2,128)(2,1)}), bf16[128,2,960]{2,1,0:T(2,128)(2,1)S(1)}, u32[]{:S(2)}, u32[]{:S(2)}) async-start(bf16[128,2,960]{2,1,0:T(2,128)(2,1)} %reshape.50), calls=%async_computation.1 | async-start | bytes 1048576 | tf_op jit(solution)/shard_map/all_to_all | solution.py:138
  189.4 0.5 all-reduce.3.cloned.1.call-update
  189.9 1.3 dynamic-slice
  191.8 191.3 %all-reduce.3.cloned.1.call-done = f32[43008]{0:T(1024)} async-done(((f32[43008]{0:T(1024)}), f32[43008]{0:T(1024)}) %all-reduce.3.cloned.1.call-update) | async-done | bytes 172048
  383.2 1.4 divide_subtract_fusion
  384.5 0.8 reshape.51
  385.3 0.7 copy.37
  386.8 0.7 copy.39
  387.9 0.7 copy.40
  (43 shorter events, 4.5 us)
Async XLA Ops:
  11.0 21.4 %copy-start.5 = (s32[2,32]{1,0:T(2,128)S(1)}, s32[2,32]{1,0:T(2,128)}, u32[]{:S(2)}) copy-start(s32[2,32]{1,0:T(2,128)} %param.17) | copy-start | bytes 772
  13.9 37.8 %all-to-all-start = ((bf16[128,2,960]{2,1,0:T(2,128)(2,1)}), bf16[128,2,960]{2,1,0:T(2,128)(2,1)S(1)}, u32[]{:S(2)}, u32[]{:S(2)}) async-start(bf16[128,2,960]{2,1,0:T(2,128)(2,1)} %reshape.48), calls=%async_computation | async-start | bytes 1048576 | tf_op jit(solution)/shard_map/all_to_all | solution.py:123
  32.4 55.2 %all-gather.4.cloned.1.call-start = ((), (), s32[]{:S(2)}) async-start(), calls=%async_computation.2 | async-start | bytes 2457600 | tf_op jit(solution)/shard_map/all_gather | solution.py:95
  52.9 1.2 copy-start.2
  59.0 63.8 %all-gather.6.cloned.1.call-start = ((), (), s32[]{:S(2)}) async-start(), calls=%async_computation.3 | async-start | bytes 1474560 | tf_op jit(solution)/shard_map/all_gather | solution.py:99
  87.6 4.0 %copy-start = (bf16[1280,768]{0,1:T(8,128)(2,1)S(1)}, bf16[1280,768]{0,1:T(8,128)(2,1)}, u32[]{:S(2)}) copy-start(bf16[1280,768]{0,1:T(8,128)(2,1)} %all-gather.4.cloned.1.call-done) | copy-start | bytes 5898244
  92.0 1.3 copy-start.1
  94.8 66.0 %all-gather.8.cloned.1.call-start = ((), (), s32[]{:S(2)}) async-start(), calls=%async_computation.4 | async-start | bytes 1474560 | tf_op jit(solution)/shard_map/all_gather | solution.py:99
  128.8 2.3 copy-start.9
  171.0 212.1 %copy-start.6 = (f32[336]{0:T(512)S(1)}, f32[336]{0:T(512)}, u32[]{:S(2)}) copy-start(f32[336]{0:T(512)} %param.19) | copy-start | bytes 4036
  171.0 212.1 %copy-start.7 = (f32[336]{0:T(512)S(1)}, f32[336]{0:T(512)}, u32[]{:S(2)}) copy-start(f32[336]{0:T(512)} %param.20) | copy-start | bytes 4036
  171.1 212.1 %copy-start.8 = (f32[336]{0:T(512)S(1)}, f32[336]{0:T(512)}, u32[]{:S(2)}) copy-start(f32[336]{0:T(512)} %param.21) | copy-start | bytes 4036
  172.9 211.6 %all-to-all-start.1 = ((bf16[128,2,960]{2,1,0:T(2,128)(2,1)}), bf16[128,2,960]{2,1,0:T(2,128)(2,1)S(1)}, u32[]{:S(2)}, u32[]{:S(2)}) async-start(bf16[128,2,960]{2,1,0:T(2,128)(2,1)} %reshape.50), calls=%async_computation.1 | async-start | bytes 1048576 | tf_op jit(solution)/shard_map/all_to_all | solution.py:138
  189.3 193.8 %all-reduce.3.cloned.1.call-start = ((), (), s32[]{:S(2)}) async-start(), calls=%async_computation.5 | async-start | bytes 344064
  385.3 1.3 copy-start.3
  386.4 1.3 copy-start.4
Sparse Core Ops, SparseCore 0:
  59.1 28.4 all-gather.3
  94.9 27.7 all-gather.5
  130.5 30.3 all-gather.7
Sparse Core Ops, SparseCore 1:
  193.0 190.0 all-reduce.2
where the time goes:
time: 396 us
  waiting for transfers between devices  296 us (75%)
  starting transfers between devices  35.2 us (9%)
  matrix products  20.7 us (5%)
  between operations  17.5 us (4%)
  local copies, waits for them, and re-layouts  14.7 us (4%)
  other arithmetic  12 us (3%)
    unnamed x5, waiting for transfers between devices  192 us
    all_gather x2, waiting for transfers between devices, gather_gram(): return lax.all_gather(gram_part, 'tensor', axis=0, tiled=True)  56.4 us
    all_gather x1, waiting for transfers between devices, gather_columns(): return lax.all_gather(column_part, 'tensor', axis=1, tiled=True)  28.6 us
    all_to_all x1, waiting for transfers between devices, per_device(): lax.all_to_all(route_rows(joint_map, joint_pieces), 'shard', split_axis=0...  18.7 us
    all_to_all x1, starting transfers between devices, per_device(): lax.all_to_all(route_rows(joint_map, joint_pieces), 'shard', split_axis=0...  18.4 us
    dot_general x4, matrix products, newton_step(): lax.dot_general(full_iterate, polynomial, (((1,), (1,)), ((), ())), prefe...  16.4 us
    all_to_all x1, starting transfers between devices, per_device(): lax.all_to_all(own_result.reshape(shards, rows_dev, block_width), 'shard'...  16.4 us
    unnamed x27, local copies, waits for them, and re-layouts  9.48 us
  transfers between devices with their start and end apart: 6, of which 5 were waited for; matrix products, arithmetic and copies ran while one was open for 1% of the time, Pallas kernels for 0%

commit v1 on v0

--- a/solution.py
+++ b/solution.py
@@ -21,6 +21,24 @@
 second_correct = 0.99407947077967
 
 
+def collect_2(value, axis, dim):
+    ways, here, step = (lax.axis_size(axis), lax.axis_index(axis), value.shape[dim])
+    lengths = [n * ways if d == dim else n for d, n in enumerate(value.shape)]
+    full = lax.dynamic_update_slice_in_dim(
+        jnp.zeros(lengths, value.dtype), value, here * step, axis=dim
+    )
+    going_up = going_down = value
+    for far in range(1, ways // 2 + 1):
+        going_up = lax.ppermute(going_up, axis, [(d, (d + 1) % ways) for d in range(ways)])
+        full = lax.dynamic_update_slice_in_dim(full, going_up, (here - far) % ways * step, axis=dim)
+        if 2 * far < ways:
+            going_down = lax.ppermute(going_down, axis, [(d, (d - 1) % ways) for d in range(ways)])
+            full = lax.dynamic_update_slice_in_dim(
+                full, going_down, (here + far) % ways * step, axis=dim
+            )
+    return full
+
+
 def owner_table(owner_list, count):
     devices = lax.broadcasted_iota(jnp.int32, (count, owner_list.shape[0]), 0)
     return (devices == owner_list[None, :]).astype(jnp.bfloat16)
@@ -96,7 +114,7 @@
 
 
 def gather_gram(gram_part):
-    return lax.all_gather(gram_part, "tensor", axis=0, tiled=True)
+    return collect_2(gram_part, "tensor", 0)
 
 
 def per_device(

time: 396 us -> 374 us (0.944)
  waiting for transfers between devices: 296 us -> 256 us
  starting transfers between devices: 35.2 us -> 53.9 us
    all_gather x2 -> x0, waiting for transfers between devices: 56.4 us -> none  [gather_gram(): return lax.all_gather(gram_part, 'tensor', axis=0, tiled=True)]
    ppermute x0 -> x6, waiting for transfers between devices: none -> 18.4 us  [the longest x4 18.4 us: collect_2(): lax.ppermute(going_up, axis, [(d, (d + 1) % ways) for d in range(ways)])]
    ppermute x0 -> x6, starting transfers between devices: none -> 17 us  [the longest x2 8.93 us: collect_2(): lax.ppermute(going_down, axis, [(d, (d - 1) % ways) for d in range(ways)])]
    unnamed x5 -> x3, waiting for transfers between devices: 192 us -> 190 us
    unnamed x27 -> x29, local copies, waits for them, and re-layouts: 9.48 us -> 7.84 us
  transfers between devices with their start and end apart: 6 -> 10, of which waited for: 5 -> 7; matrix products, arithmetic and copies ran while one was open for 1% -> 2% of each run, Pallas kernels for 0% -> 0%
where the time goes in v1:
time: 374 us; the launch traced here: 373 us
  waiting for transfers between devices  256 us (68%)
  starting transfers between devices  53.9 us (14%)
  matrix products  19.9 us (5%)
  between operations  18 us (5%)
  local copies, waits for them, and re-layouts  13.4 us (4%)
  other arithmetic  12.2 us (3%)
    unnamed x3, waiting for transfers between devices  190 us
    all_gather x1, waiting for transfers between devices, gather_columns(): return lax.all_gather(column_part, 'tensor', axis=1, tiled=True)  28.6 us
    all_to_all x1, waiting for transfers between devices, per_device(): lax.all_to_all(route_rows(joint_map, joint_pieces), 'shard', split_axis=0...  18.7 us
    all_to_all x1, starting transfers between devices, per_device(): lax.all_to_all(route_rows(joint_map, joint_pieces), 'shard', split_axis=0...  18.4 us
    ppermute x4, waiting for transfers between devices, collect_2(): lax.ppermute(going_up, axis, [(d, (d + 1) % ways) for d in range(ways)])  18.4 us
    all_to_all x1, starting transfers between devices, per_device(): lax.all_to_all(own_result.reshape(shards, rows_dev, block_width), 'shard'...  18.2 us
    dot_general x4, matrix products, newton_step(): lax.dot_general(full_iterate, polynomial, (((1,), (1,)), ((), ())), prefe...  13.2 us
    ppermute x2, starting transfers between devices, collect_2(): lax.ppermute(going_down, axis, [(d, (d - 1) % ways) for d in range(ways)])  8.93 us
  transfers between devices with their start and end apart: 10, of which 7 were waited for; matrix products, arithmetic and copies ran while one was open for 2% of the time, Pallas kernels for 0%

profile of v1, /device:TPU:1, one launch (start us, length us, event | category | flops | bytes accessed | tf_op | source)
XLA Modules:
  0.0 373.0 jit_solution(8198781889230696485)
XLA Ops:
  8.0 0.8 slice_bitcast_fusion.1
  8.8 1.0 pad_maximum_fusion
  11.0 1.3 copy.34
  12.4 1.6 reshape.48
  13.9 18.4 %all-to-all-start = ((bf16[128,2,960]{2,1,0:T(2,128)(2,1)}), bf16[128,2,960]{2,1,0:T(2,128)(2,1)S(1)}, u32[]{:S(2)}, u32[]{:S(2)}) async-start(bf16[128,2,960]{2,1,0:T(2,128)(2,1)} %reshape.48), calls=%async_computation | async-start | bytes 1048576 | tf_op jit(solution)/shard_map/all_to_all | solution.py:141
  33.1 18.7 %all-to-all-done = bf16[128,2,960]{2,1,0:T(2,128)(2,1)S(1)} async-done(((bf16[128,2,960]{2,1,0:T(2,128)(2,1)}), bf16[128,2,960]{2,1,0:T(2,128)(2,1)S(1)}, u32[]{:S(2)}, u32[]{:S(2)}) %all-to-all-start) | async-done | bytes 491552 | tf_op jit(solution)/shard_map/all_to_all | solution.py:141
  51.8 0.8 reshape.49
  53.7 5.0 %fusion.15 = (f32[1,192,1280]{2,1,0:T(8,128)}, bf16[1280,192]{0,1:T(8,128)(2,1)}, f32[1,192,1280]{2,1,0:T(8,128)}, f32[]{:T(128)}, bf16[192,1280]{1,0:T(8,128)(2,1)}) fusion(f32[1,192,1280]{2,1,0:T(8,128)S(1)} %copy-done.3, f32[1280,192]{0,1:T(8,128)S(1)} %copy.35, pred[]{:T(512)} %get-tuple-element.21, f32[1,192,1280]{2,1,0:T(8,128)} %param.16, ...), kind=kLoop, calls=%fused_computation.37 | loop fusion | flops 4177919 | bytes 5898246 | tf_op jit(solution)/shard_map/broadcast_in_dim | solution.py:174
  58.8 28.6 %all-gather.2.cloned.1.call-done = bf16[1280,768]{0,1:T(8,128)(2,1)} async-done(((bf16[1280,192]{0,1:T(8,128)(2,1)}), bf16[1280,768]{0,1:T(8,128)(2,1)}) %all-gather.2.cloned.1.call-update) | async-done | bytes 1966096 | tf_op jit(solution)/shard_map/all_gather | solution.py:113
  87.4 3.3 fusion
  91.9 1.5 constant_dynamic-update-slice_fusion.7
  93.4 2.1 collective-permute-start
  96.3 4.4 %collective-permute-start.1 = (bf16[192,768]{1,0:T(8,128)(2,1)}, bf16[192,768]{1,0:T(8,128)(2,1)S(1)}, u32[]{:S(2)}, u32[]{:S(2)}) collective-permute-start(bf16[192,768]{1,0:T(8,128)(2,1)} %get-tuple-element.39), channel_id=1, source_target_pairs={{0,3},{1,0},{2,1},{3,2},{4,7},{5,4},{6,5},{7,6},{8,11},{9,8},{10,9... | collective-permute-start | bytes 884744 | tf_op jit(solution)/shard_map/ppermute | solution.py:35
  100.6 3.8 %collective-permute-done = bf16[192,768]{1,0:T(8,128)(2,1)S(1)} collective-permute-done((bf16[192,768]{1,0:T(8,128)(2,1)}, bf16[192,768]{1,0:T(8,128)(2,1)S(1)}, u32[]{:S(2)}, u32[]{:S(2)}) %collective-permute-start) | collective-permute-done | bytes 294944 | tf_op jit(solution)/shard_map/ppermute | solution.py:32
  104.4 2.1 collective-permute-start.2
  106.5 1.7 convolution_convert_fusion.5
  108.3 6.1 %collective-permute-done.2 = bf16[192,768]{1,0:T(8,128)(2,1)S(1)} collective-permute-done((bf16[192,768]{1,0:T(8,128)(2,1)S(1)}, bf16[192,768]{1,0:T(8,128)(2,1)S(1)}, u32[]{:S(2)}, u32[]{:S(2)}) %collective-permute-start.2) | collective-permute-done | bytes 294944 | tf_op jit(solution)/shard_map/ppermute | solution.py:32
  114.4 4.1 %add_convert_fusion = bf16[1280,768]{0,1:T(8,128)(2,1)} fusion(bf16[1280,768]{0,1:T(8,128)(2,1)S(1)} %copy-done.2, bf16[768,768]{1,0:T(8,128)(2,1)S(1)} %constant_dynamic-update-slice_fusion.4), kind=kOutput, calls=%fused_computation.4 | convolution fusion | flops 2422800384 | bytes 5111808 | tf_op jit(solution)/shard_map/dot_general | solution.py:90
  118.6 2.6 constant_dynamic-update-slice_fusion.3
  121.2 1.9 collective-permute-start.3
  123.6 4.6 %collective-permute-start.4 = (bf16[192,768]{1,0:T(8,128)(2,1)S(1)}, bf16[192,768]{1,0:T(8,128)(2,1)S(1)}, u32[]{:S(2)}, u32[]{:S(2)}) collective-permute-start(bf16[192,768]{1,0:T(8,128)(2,1)S(1)} %get-tuple-element.41), channel_id=1, source_target_pairs={{0,3},{1,0},{2,1},{3,2},{4,7},{5,4},{6,5},{7,6},{8,11},{9,8},{10,9... | collective-permute-start | bytes 884744 | tf_op jit(solution)/shard_map/ppermute | solution.py:35
  128.1 2.1 collective-permute-done.3
  130.3 1.9 collective-permute-start.5
  132.6 6.4 %collective-permute-done.5 = bf16[192,768]{1,0:T(8,128)(2,1)S(1)} collective-permute-done((bf16[192,768]{1,0:T(8,128)(2,1)S(1)}, bf16[192,768]{1,0:T(8,128)(2,1)S(1)}, u32[]{:S(2)}, u32[]{:S(2)}) %collective-permute-start.5) | collective-permute-done | bytes 294944 | tf_op jit(solution)/shard_map/ppermute | solution.py:32
  139.0 6.2 %fusion.20 = f32[1280,768]{0,1:T(8,128)} fusion(bf16[1280,768]{0,1:T(8,128)(2,1)} %add_convert_fusion, bf16[768,768]{1,0:T(8,128)(2,1)S(1)} %constant_dynamic-update-slice_fusion), kind=kOutput, calls=%fused_computation.44 | convolution fusion | flops 2418868224 | bytes 7077888 | tf_op jit(solution)/shard_map/dot_general | solution.py:90
  145.2 2.4 fusion.4
  148.2 1.6 reshape.50
  149.8 18.2 %all-to-all-start.1 = ((bf16[128,2,960]{2,1,0:T(2,128)(2,1)}), bf16[128,2,960]{2,1,0:T(2,128)(2,1)S(1)}, u32[]{:S(2)}, u32[]{:S(2)}) async-start(bf16[128,2,960]{2,1,0:T(2,128)(2,1)} %reshape.50), calls=%async_computation.1 | async-start | bytes 1048576 | tf_op jit(solution)/shard_map/all_to_all | solution.py:156
  168.5 1.3 dynamic-slice
  170.4 189.6 %all-reduce.3.cloned.1.call-done = f32[43008]{0:T(1024)} async-done(((f32[43008]{0:T(1024)}), f32[43008]{0:T(1024)}) %all-reduce.3.cloned.1.call-update) | async-done | bytes 172048
  360.1 1.4 divide_subtract_fusion
  361.5 0.8 reshape.51
  (59 shorter events, 8.8 us)
Async XLA Ops:
  11.0 21.4 %copy-start.7 = (s32[2,32]{1,0:T(2,128)S(1)}, s32[2,32]{1,0:T(2,128)}, u32[]{:S(2)}) copy-start(s32[2,32]{1,0:T(2,128)} %param.17) | copy-start | bytes 772
  13.9 37.8 %all-to-all-start = ((bf16[128,2,960]{2,1,0:T(2,128)(2,1)}), bf16[128,2,960]{2,1,0:T(2,128)(2,1)S(1)}, u32[]{:S(2)}, u32[]{:S(2)}) async-start(bf16[128,2,960]{2,1,0:T(2,128)(2,1)} %reshape.48), calls=%async_computation | async-start | bytes 1048576 | tf_op jit(solution)/shard_map/all_to_all | solution.py:141
  32.4 55.0 %all-gather.2.cloned.1.call-start = ((), (), s32[]{:S(2)}) async-start(), calls=%async_computation.2 | async-start | bytes 2457600 | tf_op jit(solution)/shard_map/all_gather | solution.py:113
  52.5 1.2 copy-start.3
  87.4 4.0 %copy-start = (bf16[1280,768]{0,1:T(8,128)(2,1)S(1)}, bf16[1280,768]{0,1:T(8,128)(2,1)}, u32[]{:S(2)}) copy-start(bf16[1280,768]{0,1:T(8,128)(2,1)} %all-gather.2.cloned.1.call-done) | copy-start | bytes 5898244
  91.8 1.6 copy-start.1
  93.4 11.0 %collective-permute-start = (bf16[192,768]{1,0:T(8,128)(2,1)}, bf16[192,768]{1,0:T(8,128)(2,1)S(1)}, u32[]{:S(2)}, u32[]{:S(2)}) collective-permute-start(bf16[192,768]{1,0:T(8,128)(2,1)} %get-tuple-element.39), channel_id=1, source_target_pairs={{0,1},{1,2},{2,3},{3,0},{4,5},{5,6},{6,7},{7,4},{8,9},{9,10},{10,1... | collective-permute-start | bytes 884744 | tf_op jit(solution)/shard_map/ppermute | solution.py:32
  96.3 12.0 %collective-permute-start.1 = (bf16[192,768]{1,0:T(8,128)(2,1)}, bf16[192,768]{1,0:T(8,128)(2,1)S(1)}, u32[]{:S(2)}, u32[]{:S(2)}) collective-permute-start(bf16[192,768]{1,0:T(8,128)(2,1)} %get-tuple-element.39), channel_id=1, source_target_pairs={{0,3},{1,0},{2,1},{3,2},{4,7},{5,4},{6,5},{7,6},{8,11},{9,8},{10,9... | collective-permute-start | bytes 884744 | tf_op jit(solution)/shard_map/ppermute | solution.py:35
  104.4 10.0 %collective-permute-start.2 = (bf16[192,768]{1,0:T(8,128)(2,1)S(1)}, bf16[192,768]{1,0:T(8,128)(2,1)S(1)}, u32[]{:S(2)}, u32[]{:S(2)}) collective-permute-start(bf16[192,768]{1,0:T(8,128)(2,1)S(1)} %collective-permute-done), channel_id=1, source_target_pairs={{0,1},{1,2},{2,3},{3,0},{4,5},{5,6},{6,7},{7,4},{8,9},{9,10},{10,1... | collective-permute-start | bytes 884744 | tf_op jit(solution)/shard_map/ppermute | solution.py:32
  106.5 7.9 %copy-start.2 = (bf16[1280,768]{0,1:T(8,128)(2,1)S(1)}, bf16[1280,768]{0,1:T(8,128)(2,1)}, u32[]{:S(2)}) copy-start(bf16[1280,768]{0,1:T(8,128)(2,1)} %copy-done.1) | copy-start | bytes 5898244
  118.5 4.6 %copy-start.4 = (bf16[192,1280]{1,0:T(8,128)(2,1)S(1)}, bf16[192,1280]{1,0:T(8,128)(2,1)}, u32[]{:S(2)}) copy-start(bf16[192,1280]{1,0:T(8,128)(2,1)} %get-tuple-element.33) | copy-start | bytes 1474564
  121.2 9.1 %collective-permute-start.3 = (bf16[192,768]{1,0:T(8,128)(2,1)S(1)}, bf16[192,768]{1,0:T(8,128)(2,1)S(1)}, u32[]{:S(2)}, u32[]{:S(2)}) collective-permute-start(bf16[192,768]{1,0:T(8,128)(2,1)S(1)} %get-tuple-element.41), channel_id=1, source_target_pairs={{0,1},{1,2},{2,3},{3,0},{4,5},{5,6},{6,7},{7,4},{8,9},{9,10},{10,1... | collective-permute-start | bytes 884744 | tf_op jit(solution)/shard_map/ppermute | solution.py:32
  123.6 9.0 %collective-permute-start.4 = (bf16[192,768]{1,0:T(8,128)(2,1)S(1)}, bf16[192,768]{1,0:T(8,128)(2,1)S(1)}, u32[]{:S(2)}, u32[]{:S(2)}) collective-permute-start(bf16[192,768]{1,0:T(8,128)(2,1)S(1)} %get-tuple-element.41), channel_id=1, source_target_pairs={{0,3},{1,0},{2,1},{3,2},{4,7},{5,4},{6,5},{7,6},{8,11},{9,8},{10,9... | collective-permute-start | bytes 884744 | tf_op jit(solution)/shard_map/ppermute | solution.py:35
  130.3 8.7 %collective-permute-start.5 = (bf16[192,768]{1,0:T(8,128)(2,1)S(1)}, bf16[192,768]{1,0:T(8,128)(2,1)S(1)}, u32[]{:S(2)}, u32[]{:S(2)}) collective-permute-start(bf16[192,768]{1,0:T(8,128)(2,1)S(1)} %collective-permute-done.3), channel_id=1, source_target_pairs={{0,1},{1,2},{2,3},{3,0},{4,5},{5,6},{6,7},{7,4},{8,9},{9,10},{10,1... | collective-permute-start | bytes 884744 | tf_op jit(solution)/shard_map/ppermute | solution.py:32
  147.9 212.2 %copy-start.8 = (f32[336]{0:T(512)S(1)}, f32[336]{0:T(512)}, u32[]{:S(2)}) copy-start(f32[336]{0:T(512)} %param.19) | copy-start | bytes 4036
  147.9 212.2 %copy-start.9 = (f32[336]{0:T(512)S(1)}, f32[336]{0:T(512)}, u32[]{:S(2)}) copy-start(f32[336]{0:T(512)} %param.20) | copy-start | bytes 4036
  147.9 212.2 %copy-start.10 = (f32[336]{0:T(512)S(1)}, f32[336]{0:T(512)}, u32[]{:S(2)}) copy-start(f32[336]{0:T(512)} %param.21) | copy-start | bytes 4036
  149.8 211.7 %all-to-all-start.1 = ((bf16[128,2,960]{2,1,0:T(2,128)(2,1)}), bf16[128,2,960]{2,1,0:T(2,128)(2,1)S(1)}, u32[]{:S(2)}, u32[]{:S(2)}) async-start(bf16[128,2,960]{2,1,0:T(2,128)(2,1)} %reshape.50), calls=%async_computation.1 | async-start | bytes 1048576 | tf_op jit(solution)/shard_map/all_to_all | solution.py:156
  167.9 192.1 %all-reduce.3.cloned.1.call-start = ((), (), s32[]{:S(2)}) async-start(), calls=%async_computation.3 | async-start | bytes 344064
  362.2 1.3 copy-start.5
  363.3 1.3 copy-start.6
Sparse Core Ops, SparseCore 0:
  58.9 28.4 all-gather.1
Sparse Core Ops, SparseCore 1:
  171.7 188.3 all-reduce.2
